TPU v7x, 512 devices: a whole 4x4x16 slice. The times are simulated.
512 devices in a mesh: men: 32 (over z_lo, y, core), women: 16 (over z_hi, x).
Axes of the slice: x: 4, y: 4, z: 16 (z_hi: 4, z_lo: 4; z = z_hi * 4 + z_lo), core: 2. Of those that a mesh axis runs over, the one named last changes fastest.
Arguments:
- men_embed: bfloat16 [65536, 128], P(('men', 'women')), may hold values from -4 to 4
- women_embed: bfloat16 [16384, 128], P(('women', 'men')), may hold values from -4 to 4
- men_count: int32 [65536], P('men'), may hold values from 1 to 297, as said below
- women_count: int32 [16384], P('women'), may hold values from 1 to 299
- women_root: float32 [16384], P('women'), may hold values from 0.5 to 6, as said below
- men_cotangent: float32 [65536], P('men'), may hold values from -300 to 300
- women_cotangent: float32 [16384], P('women'), may hold values from 24 to 864, as said below
Outputs:
- men_grad: float32 [65536, 128], P(('men', 'women'))
- women_grad: float32 [16384, 128], P(('women', 'men'))
Inputs may be any that keep to these rules, and one draw needn't show every extreme that they name: `men_count`: integer masses of the male types. `women_root`: positive. `women_cotangent`: positive.
All inputs are finite; a program needn't handle non-finite values.
Results may differ from a plain program's by a relative error of at most 0.0031.
Values may be sent and summed in bfloat16 or wider, within the bound.
No kernel may reach another device: no remote copies, remote signals or barrier semaphores. Data moves between devices by JAX's collectives and lax.ppermute only.
A program may use at most 64 MiB of HBM per device.

v0:
```python
import jax
import jax.numpy as jnp
from jax import lax
from jax.sharding import PartitionSpec as P


def kernel_tile(men_rows, women_block):
    surplus = lax.dot_general(
        men_rows, women_block, (((1,), (1,)), ((), ())), preferred_element_type=jnp.float32
    )
    return jnp.exp(0.5 * surplus)


def body(
    men_embed, women_embed, men_count, women_count, women_root, men_cotangent, women_cotangent
):
    men_rows = lax.all_gather(men_embed, "women", axis=0, tiled=True)
    women_rows = lax.all_gather(women_embed, "men", axis=0, tiled=True)
    men_mass = men_count.astype(jnp.float32)
    women_mass = women_count.astype(jnp.float32)
    stored = kernel_tile(men_rows, women_rows)

    def sweep(work):
        return work(stored, women_rows, 0)

    def first_work(kernel, women_block, col_start):
        weighted = kernel * women_root[None, :]
        product = jnp.dot(
            weighted.astype(jnp.bfloat16), women_block, preferred_element_type=jnp.float32
        )
        return ((jnp.sum(weighted, axis=1), product), ())

    row_partial, weighted_v = sweep(first_work)[0]
    row_mass = lax.psum(row_partial, "women")
    men_disc = jnp.sqrt(row_mass * row_mass + 4.0 * men_mass)
    men_root = 2.0 * men_mass / (row_mass + men_disc)

    def second_work(kernel, women_block, col_start):
        return ((), (jnp.sum(kernel * men_root[:, None], axis=0),))

    col_partial = sweep(second_work)[1][0]
    col_mass = lax.psum(col_partial, "men")
    women_disc = jnp.sqrt(col_mass * col_mass + 4.0 * women_mass)
    col_grad = -women_cotangent / women_disc

    def third_work(kernel, women_block, col_start):
        weighted = kernel * col_grad[None, :]
        product = jnp.dot(
            weighted.astype(jnp.bfloat16), women_block, preferred_element_type=jnp.float32
        )
        return ((jnp.sum(weighted, axis=1), product), ())

    row_back, direct_v = sweep(third_work)[0]
    row_cot = lax.psum(row_back, "women")
    row_grad = -(men_cotangent + men_root * row_cot) / men_disc
    men_term = 0.5 * (row_grad[:, None] * weighted_v + men_root[:, None] * direct_v)
    men_grad = lax.psum_scatter(men_term, "women", scatter_dimension=0, tiled=True)

    def fourth_work(kernel, women_block, col_start):
        tangent = (
            0.5
            * kernel
            * (row_grad[:, None] * women_root[None, :] + men_root[:, None] * col_grad[None, :])
        ).astype(jnp.bfloat16)
        return (
            (),
            (
                lax.dot_general(
                    tangent, men_rows, (((0,), (0,)), ((), ())), preferred_element_type=jnp.float32
                ),
            ),
        )

    women_terms = sweep(fourth_work)[1][0]
    women_grad = lax.psum_scatter(women_terms, "men", scatter_dimension=0, tiled=True)
    return (men_grad, women_grad)


def solution(mesh):
    return jax.shard_map(
        body,
        mesh=mesh,
        in_specs=(
            P(("men", "women"), None),
            P(("women", "men"), None),
            P("men"),
            P("women"),
            P("women"),
            P("men"),
            P("women"),
        ),
        out_specs=(P(("men", "women"), None), P(("women", "men"), None)),
        check_vma=False,
    )
```

profile of v0, /device:TPU:8, one launch (start us, length us, event | category | flops | bytes accessed | tf_op | source)
XLA Modules:
  0.0 561.4 jit_solution(11899115688756769913)
XLA Ops:
  7.2 0.0 copy-start.1
  7.2 0.0 reduce-scatter.5.cloned.1.call-start
  7.2 44.3 %all_gather.7 = bf16[1024,128]{1,0:T(8,128)(2,1)S(1)} all-gather(bf16[32,128]{1,0:T(8,128)(2,1)} %param.8), channel_id=1, replica_groups=mesh['men'=32,'women'=16] {'men'}, dimensions={0}, use_global_device_ids=true | all-gather | bytes 270336 | tf_op jit(solution)/shard_map/all_gather | solution.py:18
  51.5 58.4 %all_gather.6 = bf16[2048,128]{1,0:T(8,128)(2,1)S(1)} all-gather(bf16[128,128]{1,0:T(8,128)(2,1)} %param.7), channel_id=1, replica_groups=mesh['men'=32,'women'=16] {'women'}, dimensions={0}, use_global_device_ids=true | all-gather | bytes 557056 | tf_op jit(solution)/shard_map/all_gather | solution.py:17
  109.9 4.8 multiply_reduce_fusion.2
  114.7 46.7 %psum.21 = f32[2048]{0:T(1024)S(1)} all-reduce(f32[2048]{0:T(1024)S(1)} %get-tuple-element.2), channel_id=1, replica_groups=mesh['men'=32,'women'=16] {'women'}, use_global_device_ids=true, to_apply=%region_1.0 | all-reduce | flops 2048 | bytes 16384 | tf_op jit(solution)/shard_map/psum | solution.py:34
  161.5 0.0 copy-done.1
  161.5 0.0 copy-start.2
  161.5 0.0 copy-start
  161.5 4.0 multiply_reduce_fusion
  165.5 64.6 %psum.22 = f32[1024]{0:T(1024)S(1)} all-reduce(f32[1024]{0:T(1024)S(1)} %multiply_reduce_fusion), channel_id=1, replica_groups=mesh['men'=32,'women'=16] {'men'}, use_global_device_ids=true, to_apply=%region_3.0 | all-reduce | flops 1024 | bytes 8192 | tf_op jit(solution)/shard_map/psum | solution.py:42
  230.2 0.0 copy-done.3
  230.2 0.0 copy-done.4
  230.2 4.0 multiply_reduce_fusion.1
  234.2 48.8 %psum.23 = f32[2048]{0:T(1024)S(1)} all-reduce(f32[2048]{0:T(1024)S(1)} %multiply_reduce_fusion.1), channel_id=1, replica_groups=mesh['men'=32,'women'=16] {'women'}, use_global_device_ids=true, to_apply=%region_5.0 | all-reduce | flops 2048 | bytes 16384 | tf_op jit(solution)/shard_map/psum | solution.py:54
  283.0 0.0 copy-done.2
  283.0 5.9 %fusion.4 = f32[1024,128]{1,0:T(8,128)} fusion(bf16[2048,128]{1,0:T(8,128)(2,1)S(1)} %all_gather.6, f32[2048,1024]{0,1:T(8,128)} %get-tuple-element.3, f32[2048]{0:T(1024)S(1)} %negate_divide_fusion, f32[1024]{0:T(1024)S(1)} %rsqrt_multiply_fusion, f32[2048]{0:T(1024)S(1)} %add_divide_fusion, f32[1024]{0:T(1024)S(1)} %copy-done), kind=kOutput, calls=%fused_computation.11 | convolution fusion | flops 549453824 | bytes 9461760 | tf_op jit(solution)/shard_map/dot_general | solution.py:68
  288.9 0.0 reduce-scatter.5.cloned.1.call-update
  289.0 0.0 reduce-scatter.3.cloned.1.call-start
  289.0 5.0 fusion.5
  294.0 6.1 %fusion.8 = f32[2048,128]{1,0:T(8,128)} fusion(f32[2048,128]{1,0:T(8,128)S(1)} %fusion.5, bf16[1024,128]{1,0:T(8,128)(2,1)S(1)} %all_gather.7, f32[2048,1024]{0,1:T(8,128)} %get-tuple-element.3, f32[1024]{0:T(1024)S(1)} %copy-done, f32[2048]{0:T(1024)S(1)} %negate_divide_fusion), kind=kOutput, calls=%fused_computation.15 | convolution fusion | flops 541851648 | bytes 10760192 | tf_op jit(solution)/shard_map/dot_general | solution.py:28
  300.1 0.0 reduce-scatter.3.cloned.1.call-update
  300.1 132.9 %reduce-scatter.5.cloned.1.call-done = f32[32,128]{1,0:T(8,128)} async-done(((f32[1024,128]{1,0:T(8,128)}), f32[32,128]{1,0:T(8,128)}) %reduce-scatter.5.cloned.1.call-update) | async-done | bytes 16400 | tf_op jit(solution)/shard_map/reduce_scatter | solution.py:75
  432.9 121.7 %reduce-scatter.3.cloned.1.call-done = f32[128,128]{1,0:T(8,128)} async-done(((f32[2048,128]{1,0:T(8,128)}), f32[128,128]{1,0:T(8,128)}) %reduce-scatter.3.cloned.1.call-update) | async-done | bytes 65552 | tf_op jit(solution)/shard_map/reduce_scatter | solution.py:57
  (6 shorter events, 0.0 us)
Async XLA Ops:
  7.2 154.3 %copy-start.1 = (s32[2048]{0:T(1024)S(1)}, s32[2048]{0:T(1024)}, u32[]{:S(2)}) copy-start(s32[2048]{0:T(1024)} %param.9) | copy-start | bytes 24580
  7.2 425.8 %reduce-scatter.5.cloned.1.call-start = ((), (), s32[]{:S(2)}) async-start(), calls=%async_computation.3 | async-start | bytes 540672 | tf_op jit(solution)/shard_map/reduce_scatter | solution.py:75
  109.9 120.3 %copy-start.3 = (s32[1024]{0:T(1024)S(1)}, s32[1024]{0:T(1024)}, u32[]{:S(2)}) copy-start(s32[1024]{0:T(1024)} %param.10) | copy-start | bytes 12292
  109.9 120.3 %copy-start.4 = (f32[1024]{0:T(1024)S(1)}, f32[1024]{0:T(1024)}, u32[]{:S(2)}) copy-start(f32[1024]{0:T(1024)} %param.13) | copy-start | bytes 12292
  161.5 121.5 %copy-start.2 = (f32[2048]{0:T(1024)S(1)}, f32[2048]{0:T(1024)}, u32[]{:S(2)}) copy-start(f32[2048]{0:T(1024)} %param.12) | copy-start | bytes 24580
  161.5 121.5 %copy-start = (f32[1024]{0:T(1024)S(1)}, f32[1024]{0:T(1024)}, u32[]{:S(2)}) copy-start(f32[1024]{0:T(1024)} %param.11) | copy-start | bytes 12292
  289.0 265.6 %reduce-scatter.3.cloned.1.call-start = ((), (), s32[]{:S(2)}) async-start(), calls=%async_computation.2 | async-start | bytes 1114112 | tf_op jit(solution)/shard_map/reduce_scatter | solution.py:57
Sparse Core Ops, SparseCore 0:
  289.1 143.8 reduce-scatter.4
  437.6 116.9 reduce-scatter.2
where the time goes:
time: 562 us; the launch traced here: 561 us
  blocking collectives  263 us (47%)
  waiting for transfers between devices  255 us (45%)
  matrix products  21.8 us (4%)
  between operations  14.1 us (3%)
  other arithmetic  8.05 us (1%)
    reduce_scatter x1, waiting for transfers between devices, body(): lax.psum_scatter(women_terms, 'men', scatter_dimension=0, tiled=True)  133 us
    reduce_scatter x1, waiting for transfers between devices, body(): lax.psum_scatter(men_term, 'women', scatter_dimension=0, tiled=True)  122 us
    psum x1, blocking collectives, body(): col_mass = lax.psum(col_partial, 'men')  64.6 us
    all_gather x1, blocking collectives, body(): men_rows = lax.all_gather(men_embed, 'women', axis=0, tiled=True)  58.4 us
    psum x1, blocking collectives, body(): row_cot = lax.psum(row_back, 'women')  48.8 us
    psum x1, blocking collectives, body(): row_mass = lax.psum(row_partial, 'women')  46.7 us
    all_gather x1, blocking collectives, body(): women_rows = lax.all_gather(women_embed, 'men', axis=0, tiled=True)  44.3 us
  transfers between devices with their start and end apart: 2, of which 2 were waited for; matrix products, arithmetic and copies ran while one was open for 2% of the time, Pallas kernels for 0%

commit v1 on v0

--- a/solution.py
+++ b/solution.py
@@ -1,7 +1,18 @@
+import functools
 import jax
 import jax.numpy as jnp
 from jax import lax
 from jax.sharding import PartitionSpec as P
+
+
+def do_slot(inner_x, axis_tag, dimension_no):
+    m_next = lax.all_to_all(
+        jnp.stack([inner_x for _ in range(lax.axis_size(axis_tag))]), axis_tag, 0, 0
+    )
+    return jnp.concatenate(m_next, axis=dimension_no)
+
+
+groups_test = functools.partial(do_slot, axis_tag="women", dimension_no=0)
 
 
 def kernel_tile(men_rows, women_block):
@@ -14,7 +25,7 @@
 def body(
     men_embed, women_embed, men_count, women_count, women_root, men_cotangent, women_cotangent
 ):
-    men_rows = lax.all_gather(men_embed, "women", axis=0, tiled=True)
+    men_rows = groups_test(men_embed)
     women_rows = lax.all_gather(women_embed, "men", axis=0, tiled=True)
     men_mass = men_count.astype(jnp.float32)
     women_mass = women_count.astype(jnp.float32)

time: 562 us -> 538 us (0.957)
  blocking collectives: 263 us -> 218 us
  starting transfers between devices: 0.08 us -> 17.7 us
    all_gather x1 -> x0, blocking collectives: 58.4 us -> none  [body(): men_rows = lax.all_gather(men_embed, 'women', axis=0, tiled=True)]
    all_to_all x0 -> x1, starting transfers between devices: none -> 17.7 us  [do_slot(): lax.all_to_all(jnp.stack([inner_x for _ in range(lax.axis_size(axis_tag))...]
    psum x1, blocking collectives: 46.7 us -> 61.4 us  [body(): row_mass = lax.psum(row_partial, 'women')]
  transfers between devices with their start and end apart: 2 -> 3, of which waited for: 2 -> 2; matrix products, arithmetic and copies ran while one was open for 2% -> 2% of each run, Pallas kernels for 0% -> 0%
where the time goes in v1:
time: 538 us; the launch traced here: 537 us
  waiting for transfers between devices  256 us (48%)
  blocking collectives  218 us (41%)
  matrix products  21.8 us (4%)
  starting transfers between devices  17.7 us (3%)
  between operations  14.2 us (3%)
  other arithmetic  8.05 us (1%)
    reduce_scatter x1, waiting for transfers between devices, body(): lax.psum_scatter(women_terms, 'men', scatter_dimension=0, tiled=True)  135 us
    reduce_scatter x1, waiting for transfers between devices, body(): lax.psum_scatter(men_term, 'women', scatter_dimension=0, tiled=True)  122 us
    psum x1, blocking collectives, body(): row_mass = lax.psum(row_partial, 'women')  61.4 us
    psum x1, blocking collectives, body(): col_mass = lax.psum(col_partial, 'men')  60.7 us
    all_gather x1, blocking collectives, body(): women_rows = lax.all_gather(women_embed, 'men', axis=0, tiled=True)  48.7 us
    psum x1, blocking collectives, body(): row_cot = lax.psum(row_back, 'women')  46.8 us
    all_to_all x1, starting transfers between devices, do_slot(): lax.all_to_all(jnp.stack([inner_x for _ in range(lax.axis_size(axis_tag))...  17.7 us
  transfers between devices with their start and end apart: 3, of which 2 were waited for; matrix products, arithmetic and copies ran while one was open for 2% of the time, Pallas kernels for 0%

profile of v1, /device:TPU:8, one launch (start us, length us, event | category | flops | bytes accessed | tf_op | source)
XLA Modules:
  0.0 537.5 jit_solution(1263063015736483909)
XLA Ops:
  7.2 0.0 copy-start.1
  7.2 1.7 stack.2
  8.8 17.7 %all-to-all-start = ((bf16[16,128,128]{2,1,0:T(8,128)(2,1)}), bf16[16,128,128]{2,1,0:T(8,128)(2,1)S(1)}, u32[]{:S(2)}, u32[]{:S(2)}) async-start(bf16[16,128,128]{2,1,0:T(8,128)(2,1)} %stack.2), calls=%async_computation | async-start | bytes 1048576 | tf_op jit(solution)/shard_map/all_to_all | solution.py:9
  26.5 0.0 reduce-scatter.5.cloned.1.call-start
  26.5 48.7 %all_gather.3 = bf16[1024,128]{1,0:T(8,128)(2,1)S(1)} all-gather(bf16[32,128]{1,0:T(8,128)(2,1)} %param.8), channel_id=1, replica_groups=mesh['men'=32,'women'=16] {'men'}, dimensions={0}, use_global_device_ids=true | all-gather | bytes 270336 | tf_op jit(solution)/shard_map/all_gather | solution.py:29
  75.2 0.0 all-to-all-done
  75.2 4.8 multiply_reduce_fusion.2
  80.1 61.4 %psum.21 = f32[2048]{0:T(1024)S(1)} all-reduce(f32[2048]{0:T(1024)S(1)} %get-tuple-element.2), channel_id=1, replica_groups=mesh['men'=32,'women'=16] {'women'}, use_global_device_ids=true, to_apply=%region_1.0 | all-reduce | flops 2048 | bytes 16384 | tf_op jit(solution)/shard_map/psum | solution.py:45
  141.5 0.0 copy-done.1
  141.5 0.0 copy-start.2
  141.5 0.0 copy-start
  141.6 4.0 multiply_reduce_fusion
  145.6 60.7 %psum.22 = f32[1024]{0:T(1024)S(1)} all-reduce(f32[1024]{0:T(1024)S(1)} %multiply_reduce_fusion), channel_id=1, replica_groups=mesh['men'=32,'women'=16] {'men'}, use_global_device_ids=true, to_apply=%region_3.0 | all-reduce | flops 1024 | bytes 8192 | tf_op jit(solution)/shard_map/psum | solution.py:53
  206.3 0.0 copy-done.3
  206.3 4.0 multiply_reduce_fusion.1
  210.3 46.8 %psum.23 = f32[2048]{0:T(1024)S(1)} all-reduce(f32[2048]{0:T(1024)S(1)} %multiply_reduce_fusion.1), channel_id=1, replica_groups=mesh['men'=32,'women'=16] {'women'}, use_global_device_ids=true, to_apply=%region_5.0 | all-reduce | flops 2048 | bytes 16384 | tf_op jit(solution)/shard_map/psum | solution.py:65
  257.1 5.9 %fusion.4 = f32[1024,128]{1,0:T(8,128)} fusion(bf16[2048,128]{1,0:T(8,128)(2,1)S(1)} %bitcast.7, f32[2048,1024]{0,1:T(8,128)} %get-tuple-element.3, f32[2048]{0:T(1024)S(1)} %negate_divide_fusion, f32[1024]{0:T(1024)S(1)} %rsqrt_multiply_fusion, f32[2048]{0:T(1024)S(1)} %add_divide_fusion, f32[1024]{0:T(1024)S(1)} %copy-done), kind=kOutput, calls=%fused_computation.11 | convolution fusion | flops 549453824 | bytes 9461760 | tf_op jit(solution)/shard_map/dot_general | solution.py:79
  263.0 0.0 reduce-scatter.5.cloned.1.call-update
  263.0 0.0 reduce-scatter.3.cloned.1.call-start
  263.1 5.0 fusion.5
  268.1 6.1 %fusion.8 = f32[2048,128]{1,0:T(8,128)} fusion(f32[2048,128]{1,0:T(8,128)S(1)} %fusion.5, bf16[1024,128]{1,0:T(8,128)(2,1)S(1)} %all_gather.3, f32[2048,1024]{0,1:T(8,128)} %get-tuple-element.3, f32[1024]{0:T(1024)S(1)} %copy-done, f32[2048]{0:T(1024)S(1)} %negate_divide_fusion), kind=kOutput, calls=%fused_computation.15 | convolution fusion | flops 541851648 | bytes 10760192 | tf_op jit(solution)/shard_map/dot_general | solution.py:39
  274.1 0.0 reduce-scatter.3.cloned.1.call-update
  274.2 134.7 %reduce-scatter.5.cloned.1.call-done = f32[32,128]{1,0:T(8,128)} async-done(((f32[1024,128]{1,0:T(8,128)}), f32[32,128]{1,0:T(8,128)}) %reduce-scatter.5.cloned.1.call-update) | async-done | bytes 16400 | tf_op jit(solution)/shard_map/reduce_scatter | solution.py:86
  408.9 121.7 %reduce-scatter.3.cloned.1.call-done = f32[128,128]{1,0:T(8,128)} async-done(((f32[2048,128]{1,0:T(8,128)}), f32[128,128]{1,0:T(8,128)}) %reduce-scatter.3.cloned.1.call-update) | async-done | bytes 65552 | tf_op jit(solution)/shard_map/reduce_scatter | solution.py:68
  (8 shorter events, 0.1 us)
Async XLA Ops:
  7.2 134.3 %copy-start.1 = (s32[2048]{0:T(1024)S(1)}, s32[2048]{0:T(1024)}, u32[]{:S(2)}) copy-start(s32[2048]{0:T(1024)} %param.9) | copy-start | bytes 24580
  8.8 66.4 %all-to-all-start = ((bf16[16,128,128]{2,1,0:T(8,128)(2,1)}), bf16[16,128,128]{2,1,0:T(8,128)(2,1)S(1)}, u32[]{:S(2)}, u32[]{:S(2)}) async-start(bf16[16,128,128]{2,1,0:T(8,128)(2,1)} %stack.2), calls=%async_computation | async-start | bytes 1048576 | tf_op jit(solution)/shard_map/all_to_all | solution.py:9
  26.5 382.4 %reduce-scatter.5.cloned.1.call-start = ((), (), s32[]{:S(2)}) async-start(), calls=%async_computation.4 | async-start | bytes 540672 | tf_op jit(solution)/shard_map/reduce_scatter | solution.py:86
  75.2 131.1 %copy-start.3 = (s32[1024]{0:T(1024)S(1)}, s32[1024]{0:T(1024)}, u32[]{:S(2)}) copy-start(s32[1024]{0:T(1024)} %param.10) | copy-start | bytes 12292
  75.2 131.1 %copy-start.4 = (f32[1024]{0:T(1024)S(1)}, f32[1024]{0:T(1024)}, u32[]{:S(2)}) copy-start(f32[1024]{0:T(1024)} %param.13) | copy-start | bytes 12292
  141.5 115.6 %copy-start.2 = (f32[2048]{0:T(1024)S(1)}, f32[2048]{0:T(1024)}, u32[]{:S(2)}) copy-start(f32[2048]{0:T(1024)} %param.12) | copy-start | bytes 24580
  141.5 115.6 %copy-start = (f32[1024]{0:T(1024)S(1)}, f32[1024]{0:T(1024)}, u32[]{:S(2)}) copy-start(f32[1024]{0:T(1024)} %param.11) | copy-start | bytes 12292
  263.0 267.6 %reduce-scatter.3.cloned.1.call-start = ((), (), s32[]{:S(2)}) async-start(), calls=%async_computation.3 | async-start | bytes 1114112 | tf_op jit(solution)/shard_map/reduce_scatter | solution.py:68
Sparse Core Ops, SparseCore 0:
  263.2 145.6 reduce-scatter.4
  413.5 117.0 reduce-scatter.2

commit v2 on v0

--- a/solution.py
+++ b/solution.py
@@ -31,7 +31,11 @@
         return ((jnp.sum(weighted, axis=1), product), ())
 
     row_partial, weighted_v = sweep(first_work)[0]
-    row_mass = lax.psum(row_partial, "women")
+
+    def expand_skins(block_in, a_name):
+        return jnp.sum(jax.lax.all_gather(block_in, a_name), 0)
+
+    row_mass = expand_skins(row_partial, "women")
     men_disc = jnp.sqrt(row_mass * row_mass + 4.0 * men_mass)
     men_root = 2.0 * men_mass / (row_mass + men_disc)
 

time: 562 us -> 561 us (level)
    psum x1 -> x0, blocking collectives: 46.7 us -> none  [body(): row_mass = lax.psum(row_partial, 'women')]
    all_gather x0 -> x1, blocking collectives: none -> 45.9 us  [expand_skins(): return jnp.sum(jax.lax.all_gather(block_in, a_name), 0)]
where the time goes in v2:
time: 561 us
  blocking collectives  262 us (47%)
  waiting for transfers between devices  254 us (45%)
  matrix products  21.7 us (4%)
  between operations  14.1 us (3%)
  other arithmetic  8.08 us (1%)
    reduce_scatter x1, waiting for transfers between devices, body(): lax.psum_scatter(women_terms, 'men', scatter_dimension=0, tiled=True)  133 us
    reduce_scatter x1, waiting for transfers between devices, body(): lax.psum_scatter(men_term, 'women', scatter_dimension=0, tiled=True)  122 us
    psum x1, blocking collectives, body(): col_mass = lax.psum(col_partial, 'men')  64.6 us
    all_gather x1, blocking collectives, body(): men_rows = lax.all_gather(men_embed, 'women', axis=0, tiled=True)  58.4 us
    psum x1, blocking collectives, body(): row_cot = lax.psum(row_back, 'women')  48.8 us
    all_gather x1, blocking collectives, expand_skins(): return jnp.sum(jax.lax.all_gather(block_in, a_name), 0)  45.9 us
    all_gather x1, blocking collectives, body(): women_rows = lax.all_gather(women_embed, 'men', axis=0, tiled=True)  44.3 us
  transfers between devices with their start and end apart: 2, of which 2 were waited for; matrix products, arithmetic and copies ran while one was open for 2% of the time, Pallas kernels for 0%

profile of v2, /device:TPU:8, one launch (start us, length us, event | category | flops | bytes accessed | tf_op | source)
XLA Modules:
  0.0 560.5 jit_solution(6000826547724597634)
XLA Ops:
  7.2 0.0 copy-start.1
  7.2 0.0 reduce-scatter.5.cloned.1.call-start
  7.2 44.3 %all_gather.13 = bf16[1024,128]{1,0:T(8,128)(2,1)S(1)} all-gather(bf16[32,128]{1,0:T(8,128)(2,1)} %param.8), channel_id=1, replica_groups=mesh['men'=32,'women'=16] {'men'}, dimensions={0}, use_global_device_ids=true | all-gather | bytes 270336 | tf_op jit(solution)/shard_map/all_gather | solution.py:18
  51.5 58.4 %all_gather.12 = bf16[2048,128]{1,0:T(8,128)(2,1)S(1)} all-gather(bf16[128,128]{1,0:T(8,128)(2,1)} %param.7), channel_id=1, replica_groups=mesh['men'=32,'women'=16] {'women'}, dimensions={0}, use_global_device_ids=true | all-gather | bytes 557056 | tf_op jit(solution)/shard_map/all_gather | solution.py:17
  109.9 4.8 multiply_reduce_fusion.2
  114.7 45.9 %all-gather = f32[32768]{0:T(1024)S(1)} all-gather(f32[2048]{0:T(1024)S(1)} %get-tuple-element.2), channel_id=2, replica_groups=mesh['men'=32,'women'=16] {'women'}, dimensions={0}, use_global_device_ids=true | all-gather | bytes 139264 | tf_op jit(solution)/shard_map/all_gather | solution.py:36
  160.7 0.0 copy-done.1
  160.7 0.0 copy-start.2
  160.7 0.0 copy-start
  160.7 4.0 multiply_reduce_fusion
  164.7 64.6 %psum.14 = f32[1024]{0:T(1024)S(1)} all-reduce(f32[1024]{0:T(1024)S(1)} %multiply_reduce_fusion), channel_id=1, replica_groups=mesh['men'=32,'women'=16] {'men'}, use_global_device_ids=true, to_apply=%region_3.0 | all-reduce | flops 1024 | bytes 8192 | tf_op jit(solution)/shard_map/psum | solution.py:46
  229.3 0.0 copy-done.3
  229.3 0.0 copy-done.4
  229.4 4.0 multiply_reduce_fusion.1
  233.4 48.8 %psum.15 = f32[2048]{0:T(1024)S(1)} all-reduce(f32[2048]{0:T(1024)S(1)} %multiply_reduce_fusion.1), channel_id=1, replica_groups=mesh['men'=32,'women'=16] {'women'}, use_global_device_ids=true, to_apply=%region_5.0 | all-reduce | flops 2048 | bytes 16384 | tf_op jit(solution)/shard_map/psum | solution.py:58
  282.2 0.0 copy-done.2
  282.2 5.9 %fusion.4 = f32[1024,128]{1,0:T(8,128)} fusion(bf16[2048,128]{1,0:T(8,128)(2,1)S(1)} %all_gather.12, f32[2048,1024]{0,1:T(8,128)} %get-tuple-element.3, f32[2048]{0:T(1024)S(1)} %negate_divide_fusion, f32[1024]{0:T(1024)S(1)} %rsqrt_multiply_fusion, f32[2048]{0:T(1024)S(1)} %add_divide_fusion, f32[1024]{0:T(1024)S(1)} %copy-done), kind=kOutput, calls=%fused_computation.11 | convolution fusion | flops 549453824 | bytes 9461760 | tf_op jit(solution)/shard_map/dot_general | solution.py:72
  288.1 0.0 reduce-scatter.5.cloned.1.call-update
  288.1 0.0 reduce-scatter.3.cloned.1.call-start
  288.2 5.0 fusion.5
  293.2 6.1 %fusion.8 = f32[2048,128]{1,0:T(8,128)} fusion(f32[2048,128]{1,0:T(8,128)S(1)} %fusion.5, bf16[1024,128]{1,0:T(8,128)(2,1)S(1)} %all_gather.13, f32[2048,1024]{0,1:T(8,128)} %get-tuple-element.3, f32[1024]{0:T(1024)S(1)} %copy-done, f32[2048]{0:T(1024)S(1)} %negate_divide_fusion), kind=kOutput, calls=%fused_computation.15 | convolution fusion | flops 541851648 | bytes 10760192 | tf_op jit(solution)/shard_map/dot_general | solution.py:28
  299.2 0.0 reduce-scatter.3.cloned.1.call-update
  299.2 132.7 %reduce-scatter.5.cloned.1.call-done = f32[32,128]{1,0:T(8,128)} async-done(((f32[1024,128]{1,0:T(8,128)}), f32[32,128]{1,0:T(8,128)}) %reduce-scatter.5.cloned.1.call-update) | async-done | bytes 16400 | tf_op jit(solution)/shard_map/reduce_scatter | solution.py:79
  432.0 121.7 %reduce-scatter.3.cloned.1.call-done = f32[128,128]{1,0:T(8,128)} async-done(((f32[2048,128]{1,0:T(8,128)}), f32[128,128]{1,0:T(8,128)}) %reduce-scatter.3.cloned.1.call-update) | async-done | bytes 65552 | tf_op jit(solution)/shard_map/reduce_scatter | solution.py:61
  (8 shorter events, 0.1 us)
Async XLA Ops:
  7.2 153.5 %copy-start.1 = (s32[2048]{0:T(1024)S(1)}, s32[2048]{0:T(1024)}, u32[]{:S(2)}) copy-start(s32[2048]{0:T(1024)} %param.9) | copy-start | bytes 24580
  7.2 424.8 %reduce-scatter.5.cloned.1.call-start = ((), (), s32[]{:S(2)}) async-start(), calls=%async_computation.3 | async-start | bytes 540672 | tf_op jit(solution)/shard_map/reduce_scatter | solution.py:79
  109.9 119.4 %copy-start.3 = (s32[1024]{0:T(1024)S(1)}, s32[1024]{0:T(1024)}, u32[]{:S(2)}) copy-start(s32[1024]{0:T(1024)} %param.10) | copy-start | bytes 12292
  109.9 119.4 %copy-start.4 = (f32[1024]{0:T(1024)S(1)}, f32[1024]{0:T(1024)}, u32[]{:S(2)}) copy-start(f32[1024]{0:T(1024)} %param.13) | copy-start | bytes 12292
  160.7 121.5 %copy-start.2 = (f32[2048]{0:T(1024)S(1)}, f32[2048]{0:T(1024)}, u32[]{:S(2)}) copy-start(f32[2048]{0:T(1024)} %param.12) | copy-start | bytes 24580
  160.7 121.5 %copy-start = (f32[1024]{0:T(1024)S(1)}, f32[1024]{0:T(1024)}, u32[]{:S(2)}) copy-start(f32[1024]{0:T(1024)} %param.11) | copy-start | bytes 12292
  288.1 265.6 %reduce-scatter.3.cloned.1.call-start = ((), (), s32[]{:S(2)}) async-start(), calls=%async_computation.2 | async-start | bytes 1114112 | tf_op jit(solution)/shard_map/reduce_scatter | solution.py:61
Sparse Core Ops, SparseCore 0:
  288.2 143.6 reduce-scatter.4
  436.6 117.0 reduce-scatter.2
